TPU v7x, 32 devices: a whole 2x2x4 slice. The times are simulated.
32 devices in a mesh: groups: 2 (over x), wide: 16 (over z, y, core).
Axes of the slice: x: 2, y: 2, z: 4, core: 2. Of those that a mesh axis runs over, the one named last changes fastest.
Arguments:
- query_act: bfloat16 [4096, 2048], P(('groups', 'wide')), parts along dimension 0, may hold values from -6 to 6
- query_grad: bfloat16 [4096, 4096], P(('groups', 'wide')), parts along dimension 0, may hold values from -6 to 6
- query_positions: int32 [4096], P(('groups', 'wide')), parts along dimension 0, may hold values from 0 to 4095
- act_basis: bfloat16 [2048, 1024], P(None, 'wide'), may hold values from -0.125 to 0.125
- grad_basis: bfloat16 [4096, 2048], P(None, 'wide'), may hold values from -0.09375 to 0.09375
- eig_values: bfloat16 [1024, 2048], P('wide'), may hold values from 0.05 to 50, as said below
- damping_index: int32 [12], P('groups'), parts along dimension 0, may hold values from 0 to 8
- train_act_rot: bfloat16 [1024, 6144], P(None, 'wide'), may hold values from -6 to 6
- train_grad_rot: bfloat16 [2048, 6144], P(None, 'wide'), may hold values from -6 to 6
- train_positions: int32 [6144], P('wide'), may hold values from 0 to 4095
Outputs:
- influences: float32 [12, 6144], P('groups', 'wide'), parts along dimension 0
There are 2 independent parts, one for each index of `groups`. A program takes and returns all parts, laid end to end along the dimension named above; an argument that names none is the same for every part. Nothing has to cross between parts.
Inputs may be any that keep to these rules, and one draw needn't show every extreme that they name: `eig_values`: positive corrected eigenvalues.
All inputs are finite; a program needn't handle non-finite values.
Results may differ from a plain program's by a relative error of at most 0.0059.
Values may be sent and summed in bfloat16 or wider, within the bound.
No kernel may reach another device: no remote copies, remote signals or barrier semaphores. Data moves between devices by JAX's collectives and lax.ppermute only.
A program may use at most 128 MiB of HBM per device.

v0:
```python
import math
import jax
import jax.numpy as jnp
from jax import lax
from jax.sharding import PartitionSpec as P

EIG_IN = 1024
EIG_OUT = 2048
PROMPT = 1024


def score_rows(grad_rows, eig_rows, dampings, train_act_rot, train_grad_rot):
    acts_rows = train_act_rot.astype(jnp.float32)
    grad_wide = grad_rows.astype(jnp.float32)
    eig_wide = eig_rows.astype(jnp.float32)
    results = []
    for damping in range(dampings.shape[0]):
        precond = (grad_wide / (eig_wide + dampings[damping])).astype(jnp.bfloat16)
        projected = jnp.dot(precond, train_grad_rot, preferred_element_type=jnp.float32)
        results.append(jnp.sum(projected * acts_rows, axis=0))
    return jnp.stack(results)


def shards(
    query_act,
    query_grad,
    query_positions,
    act_basis,
    grad_basis,
    eig_values,
    damping_index,
    train_act_rot,
    train_grad_rot,
    train_positions,
):
    act_full = jnp.dot(
        query_act,
        lax.all_gather(act_basis, "wide", axis=1, tiled=True),
        preferred_element_type=jnp.float32,
    )
    grad_full = jnp.dot(
        query_grad,
        lax.all_gather(grad_basis, "wide", axis=1, tiled=True),
        preferred_element_type=jnp.float32,
    )
    act_rot = act_full.astype(jnp.bfloat16)
    grad_rot = grad_full.astype(jnp.bfloat16)
    query_weight = jnp.where(query_positions >= PROMPT, 1.0, 0.0).astype(jnp.bfloat16)
    grad_kept = grad_rot * query_weight[:, None]
    eig_total = lax.psum(jnp.sum(eig_values.astype(jnp.float32)), "wide")
    mean_eig = eig_total / (EIG_IN * EIG_OUT)
    dampings = mean_eig * jnp.exp2(damping_index.astype(jnp.float32) - 4.0)
    partial_whole = lax.dot_general(
        act_rot, grad_kept, (((0,), (0,)), ((), ())), preferred_element_type=jnp.float32
    )
    query_gradient = lax.psum(partial_whole, "wide").astype(jnp.bfloat16)
    totals = score_rows(
        query_gradient,
        lax.all_gather(eig_values, "wide", axis=0, tiled=True),
        dampings,
        train_act_rot,
        train_grad_rot,
    )
    query_count = query_act.shape[0] * lax.axis_size("wide")
    factor = mean_eig * (1.0 / math.sqrt(float(query_count) * EIG_IN * EIG_OUT))
    train_weight = jnp.where(train_positions >= PROMPT, 1.0, 0.0).astype(jnp.float32)
    return totals * factor * train_weight[None, :]


def solution(mesh):
    in_specs = (
        P(("groups", "wide"), None),
        P(("groups", "wide"), None),
        P(("groups", "wide")),
        P(None, "wide"),
        P(None, "wide"),
        P("wide", None),
        P("groups"),
        P(None, "wide"),
        P(None, "wide"),
        P("wide"),
    )
    out_specs = P("groups", "wide")
    return jax.shard_map(shards, mesh=mesh, in_specs=in_specs, out_specs=out_specs, check_vma=False)
```

profile of v0, /device:TPU:1, one launch (start us, length us, event | category | flops | bytes accessed | tf_op | source)
XLA Modules:
  0.0 428.8 jit_solution(4725387925321449047)
XLA Ops:
  6.5 0.0 copy-start
  6.5 0.7 all-gather.6.cloned.1.call-update
  7.3 0.0 all-gather.4.cloned.1.call-start
  7.3 0.7 all-gather.4.cloned.1.call-update
  8.0 0.0 all-gather.8.cloned.1.call-start
  8.1 0.7 all-gather.8.cloned.1.call-update
  8.7 1.7 convert_reduce_fusion
  10.4 0.7 fusion.38
  11.1 0.7 compare_select_fusion
  11.8 130.6 %all-gather.6.cloned.1.call-done = bf16[4096,2048]{1,0:T(8,128)(2,1)} async-done(((bf16[4096,128]{1,0:T(8,128)(2,1)}), bf16[4096,2048]{1,0:T(8,128)(2,1)}) %all-gather.6.cloned.1.call-update) | async-done | bytes 16777232 | tf_op jit(solution)/shard_map/all_gather | solution.py:43
  142.4 8.4 %fusion.18 = bf16[128,2048]{1,0:T(8,128)(2,1)S(1)} fusion(bf16[128,4096]{1,0:T(8,128)(2,1)} %param.11, bf16[4096,2048]{1,0:T(8,128)(2,1)} %all-gather.6.cloned.1.call-done, bf16[128]{0:T(256)(128)(2,1)S(1)} %fusion.38), kind=kOutput, calls=%fused_computation.31 | convolution fusion | flops 2148007936 | bytes 18350336 | tf_op jit(solution)/shard_map/dot_general | solution.py:41
  150.8 42.5 %all-gather.4.cloned.1.call-done = bf16[2048,1024]{0,1:T(8,128)(2,1)} async-done(((bf16[2048,64]{0,1:T(8,128)(2,1)}), bf16[2048,1024]{0,1:T(8,128)(2,1)}) %all-gather.4.cloned.1.call-update) | async-done | bytes 4194320 | tf_op jit(solution)/shard_map/all_gather | solution.py:38
  193.3 0.0 copy-done.1
  193.3 8.1 %fusion.37 = f32[1024,2048]{1,0:T(8,128)} fusion(bf16[128,2048]{1,0:T(8,128)(2,1)S(1)} %fusion.18, bf16[128,2048]{1,0:T(8,128)(2,1)S(1)} %copy-done.1, bf16[2048,1024]{0,1:T(8,128)(2,1)} %all-gather.4.cloned.1.call-done), kind=kOutput, calls=%fused_computation.39 | convolution fusion | flops 1073872896 | bytes 13631488 | tf_op jit(solution)/shard_map/dot_general | solution.py:53
  201.4 195.6 %all-reduce.2 = (bf16[1024,2048]{1,0:T(8,128)(2,1)}, f32[]{:T(128)}) all-reduce(f32[1024,2048]{1,0:T(8,128)} %fusion.37, f32[]{:T(128)} %convert_reduce_fusion), channel_id=1, replica_groups=mesh['groups'=2,'wide'=16] {'wide'}, use_global_device_ids=true, to_apply=%region_0.1 | all-reduce | flops 2097153 | bytes 12582920 | tf_op jit(solution)/shard_map/psum | solution.py:56
  397.8 0.7 fusion.39
  398.4 0.0 copy-done.4
  398.5 7.0 %fusion.24 = f32[384]{0:T(512)S(1)} fusion(bf16[1024,384]{1,0:T(8,128)(2,1)S(1)} %copy-done.4, bf16[2048,384]{1,0:T(8,128)(2,1)S(1)} %copy-done, bf16[1024,2048]{1,0:T(8,128)(2,1)} %get-tuple-element.5, bf16[1024,2048]{1,0:T(8,128)(2,1)} %all-gather.8.cloned.1.call-done, f32[]{:T(128)} %bitcast.5), kind=kOutput, calls=%fused_computation.37 | convolution fusion | flops 1622277760 | bytes 10749444 | tf_op jit(solution)/shard_map/dot_general | solution.py:19
  405.5 3.0 fusion.23
  408.5 3.1 fusion.22
  411.6 3.0 fusion.21
  414.6 3.3 fusion.20
  417.9 3.0 fusion.19
  421.6 0.6 multiply_multiply_fusion
  (19 shorter events, 0.1 us)
Async XLA Ops:
  6.5 391.9 %copy-start = (bf16[2048,384]{1,0:T(8,128)(2,1)S(1)}, bf16[2048,384]{1,0:T(8,128)(2,1)}, u32[]{:S(2)}) copy-start(bf16[2048,384]{1,0:T(8,128)(2,1)} %param.18) | copy-start | bytes 4718596
  6.5 135.9 %all-gather.6.cloned.1.call-start = ((), (), s32[]{:S(2)}) async-start(), calls=%async_computation.1 | async-start | bytes 17825792 | tf_op jit(solution)/shard_map/all_gather | solution.py:43
  7.3 186.1 %all-gather.4.cloned.1.call-start = ((), (), s32[]{:S(2)}) async-start(), calls=%async_computation | async-start | bytes 4456448 | tf_op jit(solution)/shard_map/all_gather | solution.py:38
  8.0 390.4 %all-gather.8.cloned.1.call-start = ((), (), s32[]{:S(2)}) async-start(), calls=%async_computation.2 | async-start | bytes 4456448 | tf_op jit(solution)/shard_map/all_gather | solution.py:59
  11.8 181.6 %copy-start.1 = (bf16[128,2048]{1,0:T(8,128)(2,1)S(1)}, bf16[128,2048]{1,0:T(8,128)(2,1)}, u32[]{:S(2)}) copy-start(bf16[128,2048]{1,0:T(8,128)(2,1)} %param.10) | copy-start | bytes 1572868
  201.4 196.3 %copy-start.5 = (s32[6]{0:T(128)S(1)}, s32[6]{0:T(128)}, u32[]{:S(2)}) copy-start(s32[6]{0:T(128)} %param.16) | copy-start | bytes 76
  201.4 197.0 %copy-start.4 = (bf16[1024,384]{1,0:T(8,128)(2,1)S(1)}, bf16[1024,384]{1,0:T(8,128)(2,1)}, u32[]{:S(2)}) copy-start(bf16[1024,384]{1,0:T(8,128)(2,1)} %param.17) | copy-start | bytes 2359300
  398.4 7.0 %copy-start.2 = (bf16[1024,2048]{1,0:T(8,128)(2,1)S(1)}, bf16[1024,2048]{1,0:T(8,128)(2,1)}, u32[]{:S(2)}) copy-start(bf16[1024,2048]{1,0:T(8,128)(2,1)} %all-gather.8.cloned.1.call-done) | copy-start | bytes 12582916
  398.4 7.0 %copy-start.3 = (bf16[1024,2048]{1,0:T(8,128)(2,1)S(1)}, bf16[1024,2048]{1,0:T(8,128)(2,1)}, u32[]{:S(2)}) copy-start(bf16[1024,2048]{1,0:T(8,128)(2,1)} %get-tuple-element.5) | copy-start | bytes 12582916
Sparse Core Ops, SparseCore 0:
  9.5 132.8 all-gather.5
  144.6 48.7 all-gather.3
  195.5 67.8 all-gather.7
where the time goes:
time: 429 us
  blocking collectives  196 us (46%)
  waiting for transfers between devices  175 us (41%)
  matrix products  39 us (9%)
  between operations  14.5 us (3%)
    psum x1, blocking collectives, shards(): query_gradient = lax.psum(partial_whole, 'wide').astype(jnp.bfloat16)  196 us
    all_gather x1, waiting for transfers between devices, shards(): lax.all_gather(grad_basis, 'wide', axis=1, tiled=True)  131 us
    all_gather x1, waiting for transfers between devices, shards(): lax.all_gather(act_basis, 'wide', axis=1, tiled=True)  42.5 us
    dot_general x6, matrix products, score_rows(): jnp.dot(precond, train_grad_rot, preferred_element_type=jnp.float32)  22.4 us
  transfers between devices with their start and end apart: 3, of which 2 were waited for; matrix products, arithmetic and copies ran while one was open for 5% of the time, Pallas kernels for 0%

commit v1 on v0

--- a/solution.py
+++ b/solution.py
@@ -7,6 +7,31 @@
 EIG_IN = 1024
 EIG_OUT = 2048
 PROMPT = 1024
+
+
+def list_corner_for(content):
+    z1, carry_in, t_next = (jax.lax.axis_size("wide"), jax.lax.axis_index("wide"), content.shape[1])
+    y1 = v_now = content
+    odd = lax.dynamic_update_slice_in_dim(
+        jnp.zeros(
+            tuple((tick * z1 if rr == 1 else tick for rr, tick in enumerate(content.shape))),
+            content.dtype,
+        ),
+        content,
+        carry_in * t_next,
+        axis=1,
+    )
+    dd = 1
+    while dd < z1 // 2 + 1:
+        y1 = jax.lax.ppermute(y1, "wide", tuple(((rr, (rr + 1) % z1) for rr in range(z1))))
+        odd = lax.dynamic_update_slice_in_dim(odd, y1, (carry_in - dd) % z1 * t_next, axis=1)
+        if 2 * dd < z1:
+            v_now = jax.lax.ppermute(
+                v_now, "wide", tuple(((rr, (rr - 1) % z1) for rr in range(z1)))
+            )
+            odd = lax.dynamic_update_slice_in_dim(odd, v_now, (carry_in + dd) % z1 * t_next, axis=1)
+        dd += 1
+    return odd
 
 
 def score_rows(grad_rows, eig_rows, dampings, train_act_rot, train_grad_rot):
@@ -38,11 +63,7 @@
         lax.all_gather(act_basis, "wide", axis=1, tiled=True),
         preferred_element_type=jnp.float32,
     )
-    grad_full = jnp.dot(
-        query_grad,
-        lax.all_gather(grad_basis, "wide", axis=1, tiled=True),
-        preferred_element_type=jnp.float32,
-    )
+    grad_full = jnp.dot(query_grad, list_corner_for(grad_basis), preferred_element_type=jnp.float32)
     act_rot = act_full.astype(jnp.bfloat16)
     grad_rot = grad_full.astype(jnp.bfloat16)
     query_weight = jnp.where(query_positions >= PROMPT, 1.0, 0.0).astype(jnp.bfloat16)

time: 429 us -> 462 us (1.077)
  local copies, waits for them, and re-layouts: 0.75 us -> 32.1 us
  starting transfers between devices: 0.08 us -> 20.1 us
  blocking collectives: 196 us -> 185 us
  waiting for transfers between devices: 175 us -> 164 us
    ppermute x0 -> x15, waiting for transfers between devices: none -> 164 us  [the longest x8 102 us: list_corner_for(): jax.lax.ppermute(y1, 'wide', tuple(((rr, (rr + 1) % z1) for rr in range(z...]
    all_gather x1 -> x0, waiting for transfers between devices: 131 us -> none  [shards(): lax.all_gather(grad_basis, 'wide', axis=1, tiled=True)]
    all_gather x1, waiting for transfers between devices: 42.5 us -> 0.01 us  [shards(): lax.all_gather(act_basis, 'wide', axis=1, tiled=True)]
    dynamic_update_slice x0 -> x16, local copies, waits for them, and re-layouts: none -> 25.4 us  [the longest x8 15.1 us: list_corner_for(): lax.dynamic_update_slice_in_dim(odd, y1, (carry_in - dd) % z1 * t_next, a...]
    ppermute x0 -> x15, starting transfers between devices: none -> 20.1 us  [the longest x8 20 us: list_corner_for(): jax.lax.ppermute(y1, 'wide', tuple(((rr, (rr + 1) % z1) for rr in range(z...]
    psum x1, blocking collectives: 196 us -> 185 us  [shards(): query_gradient = lax.psum(partial_whole, 'wide').astype(jnp.bfloat16)]
    broadcast_in_dim x0 -> x1, local copies, waits for them, and re-layouts: none -> 5.98 us  [list_corner_for(): jnp.zeros(tuple((tick * z1 if rr == 1 else tick for rr, tick in enumerate...]
    dot_general x1, matrix products: 8.11 us -> 13.1 us  [shards(): lax.dot_general(act_rot, grad_kept, (((0,), (0,)), ((), ())), preferred_e...]
  transfers between devices with their start and end apart: 3 -> 17, of which waited for: 2 -> 14; matrix products, arithmetic and copies ran while one was open for 5% -> 11% of each run, Pallas kernels for 0% -> 0%
where the time goes in v1:
time: 462 us; the launch traced here: 459 us
  blocking collectives  185 us (40%)
  waiting for transfers between devices  164 us (35%)
  matrix products  39 us (8%)
  local copies, waits for them, and re-layouts  32.1 us (7%)
  starting transfers between devices  20.1 us (4%)
  between operations  15.1 us (3%)
    psum x1, blocking collectives, shards(): query_gradient = lax.psum(partial_whole, 'wide').astype(jnp.bfloat16)  185 us
    ppermute x8, waiting for transfers between devices, list_corner_for(): jax.lax.ppermute(y1, 'wide', tuple(((rr, (rr + 1) % z1) for rr in range(z...  102 us
    ppermute x7, waiting for transfers between devices, list_corner_for(): jax.lax.ppermute(v_now, 'wide', tuple(((rr, (rr - 1) % z1) for rr in rang...  62.1 us
    dot_general x6, matrix products, score_rows(): jnp.dot(precond, train_grad_rot, preferred_element_type=jnp.float32)  22.1 us
    ppermute x8, starting transfers between devices, list_corner_for(): jax.lax.ppermute(y1, 'wide', tuple(((rr, (rr + 1) % z1) for rr in range(z...  20 us
    dynamic_update_slice x8, local copies, waits for them, and re-layouts, list_corner_for(): lax.dynamic_update_slice_in_dim(odd, y1, (carry_in - dd) % z1 * t_next, a...  15.1 us
    dot_general x1, matrix products, shards(): lax.dot_general(act_rot, grad_kept, (((0,), (0,)), ((), ())), preferred_e...  13.1 us
  transfers between devices with their start and end apart: 17, of which 14 were waited for; matrix products, arithmetic and copies ran while one was open for 11% of the time, Pallas kernels for 0%

profile of v1, /device:TPU:1, one launch (start us, length us, event | category | flops | bytes accessed | tf_op | source)
XLA Modules:
  0.0 459.0 jit_solution(10603701614874816364)
XLA Ops:
  10.0 26.1 %collective-permute-done = bf16[4096,128]{1,0:T(8,128)(2,1)} collective-permute-done((bf16[4096,128]{1,0:T(8,128)(2,1)}, bf16[4096,128]{1,0:T(8,128)(2,1)}, u32[]{:S(2)}, u32[]{:S(2)}) %collective-permute-start) | collective-permute-done | bytes 1048608 | tf_op jit(solution)/shard_map/ppermute | solution.py:26
  38.6 11.2 %collective-permute-done.1 = bf16[4096,128]{1,0:T(8,128)(2,1)} collective-permute-done((bf16[4096,128]{1,0:T(8,128)(2,1)}, bf16[4096,128]{1,0:T(8,128)(2,1)}, u32[]{:S(2)}, u32[]{:S(2)}) %collective-permute-start.1) | collective-permute-done | bytes 1048608 | tf_op jit(solution)/shard_map/ppermute | solution.py:29
  50.1 22.3 %collective-permute-done.2 = bf16[4096,128]{1,0:T(8,128)(2,1)} collective-permute-done((bf16[4096,128]{1,0:T(8,128)(2,1)}, bf16[4096,128]{1,0:T(8,128)(2,1)}, u32[]{:S(2)}, u32[]{:S(2)}) %collective-permute-start.2) | collective-permute-done | bytes 1048608 | tf_op jit(solution)/shard_map/ppermute | solution.py:26
  76.2 8.8 %collective-permute-done.3 = bf16[4096,128]{1,0:T(8,128)(2,1)S(1)} collective-permute-done((bf16[4096,128]{1,0:T(8,128)(2,1)}, bf16[4096,128]{1,0:T(8,128)(2,1)S(1)}, u32[]{:S(2)}, u32[]{:S(2)}) %collective-permute-start.3) | collective-permute-done | bytes 1048608 | tf_op jit(solution)/shard_map/ppermute | solution.py:29
  86.7 6.0 %broadcast_in_dim.21 = bf16[4096,2048]{1,0:T(8,128)(2,1)} broadcast(bf16[]{:T(256)} %constant.100.clone.1), dimensions={} | broadcast | bytes 16777218 | tf_op jit(solution)/shard_map/broadcast_in_dim | solution.py:16
  93.8 4.3 collective-permute-done.4
  102.9 10.7 %collective-permute-done.5 = bf16[4096,128]{1,0:T(8,128)(2,1)S(1)} collective-permute-done((bf16[4096,128]{1,0:T(8,128)(2,1)S(1)}, bf16[4096,128]{1,0:T(8,128)(2,1)S(1)}, u32[]{:S(2)}, u32[]{:S(2)}) %collective-permute-start.5) | collective-permute-done | bytes 1048608 | tf_op jit(solution)/shard_map/ppermute | solution.py:29
  118.4 8.3 %collective-permute-done.6 = bf16[4096,128]{1,0:T(8,128)(2,1)S(1)} collective-permute-done((bf16[4096,128]{1,0:T(8,128)(2,1)}, bf16[4096,128]{1,0:T(8,128)(2,1)S(1)}, u32[]{:S(2)}, u32[]{:S(2)}) %collective-permute-start.6) | collective-permute-done | bytes 1048608 | tf_op jit(solution)/shard_map/ppermute | solution.py:26
  130.2 19.1 %collective-permute-done.7 = bf16[4096,128]{1,0:T(8,128)(2,1)S(1)} collective-permute-done((bf16[4096,128]{1,0:T(8,128)(2,1)S(1)}, bf16[4096,128]{1,0:T(8,128)(2,1)S(1)}, u32[]{:S(2)}, u32[]{:S(2)}) %collective-permute-start.7) | collective-permute-done | bytes 1048608 | tf_op jit(solution)/shard_map/ppermute | solution.py:29
  152.7 8.7 %collective-permute-done.8 = bf16[4096,128]{1,0:T(8,128)(2,1)S(1)} collective-permute-done((bf16[4096,128]{1,0:T(8,128)(2,1)S(1)}, bf16[4096,128]{1,0:T(8,128)(2,1)S(1)}, u32[]{:S(2)}, u32[]{:S(2)}) %collective-permute-start.8) | collective-permute-done | bytes 1048608 | tf_op jit(solution)/shard_map/ppermute | solution.py:26
  165.1 4.8 %collective-permute-done.9 = bf16[4096,128]{1,0:T(8,128)(2,1)S(1)} collective-permute-done((bf16[4096,128]{1,0:T(8,128)(2,1)S(1)}, bf16[4096,128]{1,0:T(8,128)(2,1)S(1)}, u32[]{:S(2)}, u32[]{:S(2)}) %collective-permute-start.9) | collective-permute-done | bytes 1048608 | tf_op jit(solution)/shard_map/ppermute | solution.py:29
  172.1 14.8 %collective-permute-done.10 = bf16[4096,128]{1,0:T(8,128)(2,1)S(1)} collective-permute-done((bf16[4096,128]{1,0:T(8,128)(2,1)S(1)}, bf16[4096,128]{1,0:T(8,128)(2,1)S(1)}, u32[]{:S(2)}, u32[]{:S(2)}) %collective-permute-start.10) | collective-permute-done | bytes 1048608 | tf_op jit(solution)/shard_map/ppermute | solution.py:26
  190.5 7.4 %collective-permute-done.11 = bf16[4096,128]{1,0:T(8,128)(2,1)S(1)} collective-permute-done((bf16[4096,128]{1,0:T(8,128)(2,1)S(1)}, bf16[4096,128]{1,0:T(8,128)(2,1)S(1)}, u32[]{:S(2)}, u32[]{:S(2)}) %collective-permute-start.11) | collective-permute-done | bytes 1048608 | tf_op jit(solution)/shard_map/ppermute | solution.py:29
  200.2 12.2 %collective-permute-done.12 = bf16[4096,128]{1,0:T(8,128)(2,1)} collective-permute-done((bf16[4096,128]{1,0:T(8,128)(2,1)S(1)}, bf16[4096,128]{1,0:T(8,128)(2,1)}, u32[]{:S(2)}, u32[]{:S(2)}) %collective-permute-start.12) | collective-permute-done | bytes 1048608 | tf_op jit(solution)/shard_map/ppermute | solution.py:26
  218.5 3.7 convolution_convert_fusion.1
  222.2 4.9 %collective-permute-done.14 = bf16[4096,128]{1,0:T(8,128)(2,1)} collective-permute-done((bf16[4096,128]{1,0:T(8,128)(2,1)}, bf16[4096,128]{1,0:T(8,128)(2,1)}, u32[]{:S(2)}, u32[]{:S(2)}) %collective-permute-start.14) | collective-permute-done | bytes 1048608 | tf_op jit(solution)/shard_map/ppermute | solution.py:26
  229.4 13.1 %fusion.37 = f32[1024,2048]{1,0:T(8,128)} fusion(bf16[128,1024]{1,0:T(8,128)(2,1)S(1)} %convolution_convert_fusion.1, bf16[4096,2048]{1,0:T(8,128)(2,1)} %constant_dynamic-update-slice_fusion, bf16[128,4096]{1,0:T(8,128)(2,1)S(1)} %copy-done.1, bf16[128]{0:T(256)(128)(2,1)S(1)} %fusion.39), kind=kOutput, calls=%fused_computation.38 | convolution fusion | flops 2684878848 | bytes 26476800 | tf_op jit(solution)/shard_map/dot_general | solution.py:74
  242.6 184.6 %all-reduce.2 = (bf16[1024,2048]{1,0:T(8,128)(2,1)}, f32[]{:T(128)}) all-reduce(f32[1024,2048]{1,0:T(8,128)} %fusion.37, f32[]{:T(128)} %convert_reduce_fusion), channel_id=1, replica_groups=mesh['groups'=2,'wide'=16] {'wide'}, use_global_device_ids=true, to_apply=%region_0.1 | all-reduce | flops 2097153 | bytes 12582920 | tf_op jit(solution)/shard_map/psum | solution.py:77
  428.6 7.1 %fusion.24 = f32[384]{0:T(512)S(1)} fusion(bf16[1024,384]{1,0:T(8,128)(2,1)S(1)} %copy-done.6, bf16[2048,384]{1,0:T(8,128)(2,1)S(1)} %copy-done, bf16[1024,2048]{1,0:T(8,128)(2,1)} %get-tuple-element.5, bf16[1024,2048]{1,0:T(8,128)(2,1)} %all-gather.5.cloned.1.call-done, f32[]{:T(128)} %bitcast.5), kind=kOutput, calls=%fused_computation.37 | convolution fusion | flops 1622277760 | bytes 10749444 | tf_op jit(solution)/shard_map/dot_general | solution.py:44
  435.7 3.0 fusion.23
  438.7 3.0 fusion.22
  441.7 2.9 fusion.21
  444.6 3.3 fusion.20
  447.9 2.9 fusion.19
  (67 shorter events, 50.6 us)
Async XLA Ops:
  6.5 422.0 %copy-start = (bf16[2048,384]{1,0:T(8,128)(2,1)S(1)}, bf16[2048,384]{1,0:T(8,128)(2,1)}, u32[]{:S(2)}) copy-start(bf16[2048,384]{1,0:T(8,128)(2,1)} %param.18) | copy-start | bytes 4718596
  6.5 211.9 %all-gather.3.cloned.1.call-start = ((), (), s32[]{:S(2)}) async-start(), calls=%async_computation | async-start | bytes 4456448 | tf_op jit(solution)/shard_map/all_gather | solution.py:63
  7.3 421.3 %all-gather.5.cloned.1.call-start = ((), (), s32[]{:S(2)}) async-start(), calls=%async_computation.1 | async-start | bytes 4456448 | tf_op jit(solution)/shard_map/all_gather | solution.py:80
  7.3 28.8 %collective-permute-start = (bf16[4096,128]{1,0:T(8,128)(2,1)}, bf16[4096,128]{1,0:T(8,128)(2,1)}, u32[]{:S(2)}, u32[]{:S(2)}) collective-permute-start(bf16[4096,128]{1,0:T(8,128)(2,1)} %param.14), channel_id=1, source_target_pairs={{0,1},{1,2},{2,3},{3,4},{4,5},{5,6},{6,7},{7,8},{8,9},{9,10},{10,1... | collective-permute-start | bytes 3145736 | tf_op jit(solution)/shard_map/ppermute | solution.py:26
  10.0 39.8 %collective-permute-start.1 = (bf16[4096,128]{1,0:T(8,128)(2,1)}, bf16[4096,128]{1,0:T(8,128)(2,1)}, u32[]{:S(2)}, u32[]{:S(2)}) collective-permute-start(bf16[4096,128]{1,0:T(8,128)(2,1)} %param.14), channel_id=1, source_target_pairs={{0,15},{1,0},{2,1},{3,2},{4,3},{5,4},{6,5},{7,6},{8,7},{9,8},{10,9... | collective-permute-start | bytes 3145736 | tf_op jit(solution)/shard_map/ppermute | solution.py:29
  36.1 36.2 %collective-permute-start.2 = (bf16[4096,128]{1,0:T(8,128)(2,1)}, bf16[4096,128]{1,0:T(8,128)(2,1)}, u32[]{:S(2)}, u32[]{:S(2)}) collective-permute-start(bf16[4096,128]{1,0:T(8,128)(2,1)} %collective-permute-done), channel_id=1, source_target_pairs={{0,1},{1,2},{2,3},{3,4},{4,5},{5,6},{6,7},{7,8},{8,9},{9,10},{10,1... | collective-permute-start | bytes 3145736 | tf_op jit(solution)/shard_map/ppermute | solution.py:26
  49.8 35.2 %collective-permute-start.3 = (bf16[4096,128]{1,0:T(8,128)(2,1)}, bf16[4096,128]{1,0:T(8,128)(2,1)S(1)}, u32[]{:S(2)}, u32[]{:S(2)}) collective-permute-start(bf16[4096,128]{1,0:T(8,128)(2,1)} %collective-permute-done.1), channel_id=1, source_target_pairs={{0,15},{1,0},{2,1},{3,2},{4,3},{5,4},{6,5},{7,6},{8,7},{9,8},{10,9... | collective-permute-start | bytes 3145736 | tf_op jit(solution)/shard_map/ppermute | solution.py:29
  72.3 25.8 %collective-permute-start.4 = (bf16[4096,128]{1,0:T(8,128)(2,1)}, bf16[4096,128]{1,0:T(8,128)(2,1)}, u32[]{:S(2)}, u32[]{:S(2)}) collective-permute-start(bf16[4096,128]{1,0:T(8,128)(2,1)} %collective-permute-done.2), channel_id=1, source_target_pairs={{0,1},{1,2},{2,3},{3,4},{4,5},{5,6},{6,7},{7,8},{8,9},{9,10},{10,1... | collective-permute-start | bytes 3145736 | tf_op jit(solution)/shard_map/ppermute | solution.py:26
  85.0 28.7 %collective-permute-start.5 = (bf16[4096,128]{1,0:T(8,128)(2,1)S(1)}, bf16[4096,128]{1,0:T(8,128)(2,1)S(1)}, u32[]{:S(2)}, u32[]{:S(2)}) collective-permute-start(bf16[4096,128]{1,0:T(8,128)(2,1)S(1)} %collective-permute-done.3), channel_id=1, source_target_pairs={{0,15},{1,0},{2,1},{3,2},{4,3},{5,4},{6,5},{7,6},{8,7},{9,8},{10,9... | collective-permute-start | bytes 3145736 | tf_op jit(solution)/shard_map/ppermute | solution.py:29
  98.1 28.6 %collective-permute-start.6 = (bf16[4096,128]{1,0:T(8,128)(2,1)}, bf16[4096,128]{1,0:T(8,128)(2,1)S(1)}, u32[]{:S(2)}, u32[]{:S(2)}) collective-permute-start(bf16[4096,128]{1,0:T(8,128)(2,1)} %collective-permute-done.4), channel_id=1, source_target_pairs={{0,1},{1,2},{2,3},{3,4},{4,5},{5,6},{6,7},{7,8},{8,9},{9,10},{10,1... | collective-permute-start | bytes 3145736 | tf_op jit(solution)/shard_map/ppermute | solution.py:26
  113.6 35.7 %collective-permute-start.7 = (bf16[4096,128]{1,0:T(8,128)(2,1)S(1)}, bf16[4096,128]{1,0:T(8,128)(2,1)S(1)}, u32[]{:S(2)}, u32[]{:S(2)}) collective-permute-start(bf16[4096,128]{1,0:T(8,128)(2,1)S(1)} %collective-permute-done.5), channel_id=1, source_target_pairs={{0,15},{1,0},{2,1},{3,2},{4,3},{5,4},{6,5},{7,6},{8,7},{9,8},{10,9... | collective-permute-start | bytes 3145736 | tf_op jit(solution)/shard_map/ppermute | solution.py:29
  126.7 34.8 %collective-permute-start.8 = (bf16[4096,128]{1,0:T(8,128)(2,1)S(1)}, bf16[4096,128]{1,0:T(8,128)(2,1)S(1)}, u32[]{:S(2)}, u32[]{:S(2)}) collective-permute-start(bf16[4096,128]{1,0:T(8,128)(2,1)S(1)} %collective-permute-done.6), channel_id=1, source_target_pairs={{0,1},{1,2},{2,3},{3,4},{4,5},{5,6},{6,7},{7,8},{8,9},{9,10},{10,1... | collective-permute-start | bytes 3145736 | tf_op jit(solution)/shard_map/ppermute | solution.py:26
  149.3 20.6 %collective-permute-start.9 = (bf16[4096,128]{1,0:T(8,128)(2,1)S(1)}, bf16[4096,128]{1,0:T(8,128)(2,1)S(1)}, u32[]{:S(2)}, u32[]{:S(2)}) collective-permute-start(bf16[4096,128]{1,0:T(8,128)(2,1)S(1)} %collective-permute-done.7), channel_id=1, source_target_pairs={{0,15},{1,0},{2,1},{3,2},{4,3},{5,4},{6,5},{7,6},{8,7},{9,8},{10,9... | collective-permute-start | bytes 3145736 | tf_op jit(solution)/shard_map/ppermute | solution.py:29
  152.7 65.7 %copy-start.3 = (bf16[128,2048]{1,0:T(8,128)(2,1)S(1)}, bf16[128,2048]{1,0:T(8,128)(2,1)}, u32[]{:S(2)}) copy-start(bf16[128,2048]{1,0:T(8,128)(2,1)} %param.10) | copy-start | bytes 1572868
  161.5 25.5 %collective-permute-start.10 = (bf16[4096,128]{1,0:T(8,128)(2,1)S(1)}, bf16[4096,128]{1,0:T(8,128)(2,1)S(1)}, u32[]{:S(2)}, u32[]{:S(2)}) collective-permute-start(bf16[4096,128]{1,0:T(8,128)(2,1)S(1)} %collective-permute-done.8), channel_id=1, source_target_pairs={{0,1},{1,2},{2,3},{3,4},{4,5},{5,6},{6,7},{7,8},{8,9},{9,10},{10,1... | collective-permute-start | bytes 3145736 | tf_op jit(solution)/shard_map/ppermute | solution.py:26
  169.9 28.1 %collective-permute-start.11 = (bf16[4096,128]{1,0:T(8,128)(2,1)S(1)}, bf16[4096,128]{1,0:T(8,128)(2,1)S(1)}, u32[]{:S(2)}, u32[]{:S(2)}) collective-permute-start(bf16[4096,128]{1,0:T(8,128)(2,1)S(1)} %collective-permute-done.9), channel_id=1, source_target_pairs={{0,15},{1,0},{2,1},{3,2},{4,3},{5,4},{6,5},{7,6},{8,7},{9,8},{10,9... | collective-permute-start | bytes 3145736 | tf_op jit(solution)/shard_map/ppermute | solution.py:29
  172.1 57.3 %copy-start.1 = (bf16[128,4096]{1,0:T(8,128)(2,1)S(1)}, bf16[128,4096]{1,0:T(8,128)(2,1)}, u32[]{:S(2)}) copy-start(bf16[128,4096]{1,0:T(8,128)(2,1)} %param.11) | copy-start | bytes 3145732
  186.9 25.5 %collective-permute-start.12 = (bf16[4096,128]{1,0:T(8,128)(2,1)S(1)}, bf16[4096,128]{1,0:T(8,128)(2,1)}, u32[]{:S(2)}, u32[]{:S(2)}) collective-permute-start(bf16[4096,128]{1,0:T(8,128)(2,1)S(1)} %collective-permute-done.10), channel_id=1, source_target_pairs={{0,1},{1,2},{2,3},{3,4},{4,5},{5,6},{6,7},{7,8},{8,9},{9,10},{10,1... | collective-permute-start | bytes 3145736 | tf_op jit(solution)/shard_map/ppermute | solution.py:26
  197.9 19.4 %collective-permute-start.13 = (bf16[4096,128]{1,0:T(8,128)(2,1)S(1)}, bf16[4096,128]{1,0:T(8,128)(2,1)S(1)}, u32[]{:S(2)}, u32[]{:S(2)}) collective-permute-start(bf16[4096,128]{1,0:T(8,128)(2,1)S(1)} %collective-permute-done.11), channel_id=1, source_target_pairs={{0,15},{1,0},{2,1},{3,2},{4,3},{5,4},{6,5},{7,6},{8,7},{9,8},{10,9... | collective-permute-start | bytes 3145736 | tf_op jit(solution)/shard_map/ppermute | solution.py:29
  212.4 14.6 %collective-permute-start.14 = (bf16[4096,128]{1,0:T(8,128)(2,1)}, bf16[4096,128]{1,0:T(8,128)(2,1)}, u32[]{:S(2)}, u32[]{:S(2)}) collective-permute-start(bf16[4096,128]{1,0:T(8,128)(2,1)} %collective-permute-done.12), channel_id=1, source_target_pairs={{0,1},{1,2},{2,3},{3,4},{4,5},{5,6},{6,7},{7,8},{8,9},{9,10},{10,1... | collective-permute-start | bytes 3145736 | tf_op jit(solution)/shard_map/ppermute | solution.py:26
  242.6 185.3 %copy-start.7 = (s32[6]{0:T(128)S(1)}, s32[6]{0:T(128)}, u32[]{:S(2)}) copy-start(s32[6]{0:T(128)} %param.16) | copy-start | bytes 76
  242.6 186.0 %copy-start.6 = (bf16[1024,384]{1,0:T(8,128)(2,1)S(1)}, bf16[1024,384]{1,0:T(8,128)(2,1)}, u32[]{:S(2)}) copy-start(bf16[1024,384]{1,0:T(8,128)(2,1)} %param.17) | copy-start | bytes 2359300
  428.6 7.1 %copy-start.4 = (bf16[1024,2048]{1,0:T(8,128)(2,1)S(1)}, bf16[1024,2048]{1,0:T(8,128)(2,1)}, u32[]{:S(2)}) copy-start(bf16[1024,2048]{1,0:T(8,128)(2,1)} %all-gather.5.cloned.1.call-done) | copy-start | bytes 12582916
  428.6 7.1 %copy-start.5 = (bf16[1024,2048]{1,0:T(8,128)(2,1)S(1)}, bf16[1024,2048]{1,0:T(8,128)(2,1)}, u32[]{:S(2)}) copy-start(bf16[1024,2048]{1,0:T(8,128)(2,1)} %get-tuple-element.5) | copy-start | bytes 12582916
  (1 other events, 6.0 us)
Sparse Core Ops, SparseCore 0:
  9.5 80.4 all-gather.2
  92.2 68.2 all-gather.4
